TPU v7x, 32 devices: a whole 2x2x4 slice. The times are simulated.
32 devices in a mesh: dp: 16 (over z, y, x), lat: 2 (over core).
Axes of the slice: x: 2, y: 2, z: 4, core: 2. Of those that a mesh axis runs over, the one named last changes fastest.
Arguments:
- acts: bfloat16 [2048, 8192], P('dp', 'lat'), may hold values from -6 to 6
- owner_ids: int32 [2048, 4], P('dp'), may hold values from 0 to 31, all different within a row; in each aligned block of 128 rows (0 to 127, 128 to 255, ...) at most 32 rows name the same one
- block_codes: int32 [2048, 4], P('dp'), may hold values from 1 to 3
- weights: bfloat16 [4096, 8192], P(('dp', 'lat')), may hold values from -0.25 to 0.25
- enc_bias: float32 [4096], P(('dp', 'lat')), may hold values from -3 to 3
- dec_bias: float32 [8192], P('lat'), may hold values from -3 to 3
Outputs:
- recon: bfloat16 [2048, 8192], P('dp', 'lat')
- grad_weights: bfloat16 [4096, 8192], P(('dp', 'lat'))
- grad_enc_bias: float32 [4096], P(('dp', 'lat'))
- grad_dec_bias: float32 [8192], P('lat')
Inputs may be any that keep to these rules, and one draw needn't show every extreme that they name: `owner_ids`: each row names 4 different devices; in each aligned block of 128 rows (the rows of one index of dp) no device is named by more than 32 rows, and some device is named by exactly 32. `block_codes`: bit j (j < 2) of an entry says whether block j of that device's 2 blocks is active for the token.
All inputs are finite; a program needn't handle non-finite values.
Results may differ from a plain program's by a relative error of at most 0.0056.
Values may be sent and summed in bfloat16 or wider, within the bound.
No kernel may reach another device: no remote copies, remote signals or barrier semaphores. Data moves between devices by JAX's collectives and lax.ppermute only.
A program may use at most 192 MiB of HBM per device.

v0:
```python
import jax
import jax.numpy as jnp
from jax import lax
from jax.sharding import PartitionSpec as P

BLK_DEV = 2


def owner_work(rows, gate, weights, enc_bias, block_width):
    pre = (
        lax.dot_general(rows, weights, (((1,), (1,)), ((), ())), preferred_element_type=jnp.float32)
        + enc_bias[None, :]
    )
    gate_lat = jnp.repeat(gate.astype(jnp.float32), block_width, axis=1)
    codes = (jnp.maximum(pre, 0.0) * gate_lat).astype(jnp.bfloat16)
    parts = jnp.dot(codes, weights, preferred_element_type=jnp.float32).astype(jnp.bfloat16)
    return (pre, gate_lat, codes, parts)


def owner_grads(rows, errors, weights, pre, gate_lat, codes):
    gcodes = lax.dot_general(
        errors, weights, (((1,), (1,)), ((), ())), preferred_element_type=jnp.float32
    )
    gpre = gcodes * gate_lat * (pre > 0.0).astype(jnp.float32)
    grad_w = lax.dot_general(
        codes, errors, (((0,), (0,)), ((), ())), preferred_element_type=jnp.float32
    )
    grad_w = grad_w + lax.dot_general(
        gpre.astype(jnp.bfloat16),
        rows,
        (((0,), (0,)), ((), ())),
        preferred_element_type=jnp.float32,
    )
    return (grad_w.astype(jnp.bfloat16), jnp.sum(gpre, axis=0))


def slot_tables(owner_ids, block_codes, owner_total, slot_cap, blk_count):
    tok_rows, own_count = owner_ids.shape
    onehot = (
        owner_ids[:, :, None] == jnp.arange(owner_total, dtype=jnp.int32)[None, None, :]
    ).astype(jnp.float32)
    present = jnp.sum(onehot, axis=1)
    lower = (jnp.arange(tok_rows)[None, :] < jnp.arange(tok_rows)[:, None]).astype(jnp.float32)
    before = jnp.dot(lower, present, precision=lax.Precision.HIGHEST)
    slot_of = jnp.sum(onehot * before[:, None, :], axis=2)
    slot_hit = (
        slot_of[:, :, None] == jnp.arange(slot_cap, dtype=jnp.float32)[None, None, :]
    ).astype(jnp.float32)
    select = (onehot[:, :, :, None] * slot_hit[:, :, None, :]).reshape(
        tok_rows, own_count, owner_total * slot_cap
    )
    place = jnp.sum(select, axis=1)
    bits = jnp.stack([block_codes // 2**j % 2 for j in range(blk_count)], axis=-1).astype(
        jnp.float32
    )
    gates = jnp.einsum("tks,tkj->sj", select, bits)
    return (place, gates)


def local(acts, owner_ids, block_codes, weights, enc_bias, dec_bias):
    dp_count = lax.axis_size("dp")
    lat_count = lax.axis_size("lat")
    owner_total = dp_count * lat_count
    tok_rows, own_count = owner_ids.shape
    full_width = weights.shape[1]
    blk_count = BLK_DEV
    block_width = weights.shape[0] // blk_count
    slot_cap = max(2, 2 * tok_rows * own_count // owner_total)
    place, gates = slot_tables(owner_ids, block_codes, owner_total, slot_cap, blk_count)
    lat_hit = (jnp.arange(lat_count, dtype=jnp.int32) == lax.axis_index("lat")).astype(jnp.float32)
    mine = jnp.einsum(
        "tdlc,l->tdc", place.reshape(tok_rows, dp_count, lat_count, slot_cap), lat_hit
    )
    mine_b = mine.reshape(tok_rows, dp_count * slot_cap).astype(jnp.bfloat16)
    mine_gate = jnp.einsum(
        "dlcj,l->dcj", gates.reshape(dp_count, lat_count, slot_cap, blk_count), lat_hit
    )
    whole = lax.all_gather(acts, "lat", axis=1, tiled=True)
    sent = lax.dot_general(
        mine_b, whole, (((0,), (0,)), ((), ())), preferred_element_type=jnp.float32
    )
    sent = sent.astype(jnp.bfloat16).reshape(dp_count, slot_cap, full_width)
    got_rows, got_gate = (
        lax.all_to_all(sent, "dp", split_axis=0, concat_axis=0, tiled=True),
        lax.all_to_all(
            mine_gate.astype(jnp.bfloat16), "dp", split_axis=0, concat_axis=0, tiled=True
        ),
    )
    rows = got_rows.reshape(dp_count * slot_cap, full_width)
    gate = got_gate.reshape(dp_count * slot_cap, blk_count)
    pre, gate_lat, codes, parts = owner_work(rows, gate, weights, enc_bias, block_width)
    back = lax.all_to_all(
        parts.reshape(dp_count, slot_cap, full_width), "dp", split_axis=0, concat_axis=0, tiled=True
    )
    partial_value = jnp.dot(
        mine_b, back.reshape(dp_count * slot_cap, full_width), preferred_element_type=jnp.float32
    )
    summed = lax.psum_scatter(partial_value, "lat", scatter_dimension=1, tiled=True)
    full = dec_bias[None, :] + summed
    err = full - acts.astype(jnp.float32)
    gerr = err.astype(jnp.bfloat16)
    err_whole = lax.all_gather(gerr, "lat", axis=1, tiled=True)
    err_sent = lax.dot_general(
        mine_b, err_whole, (((0,), (0,)), ((), ())), preferred_element_type=jnp.float32
    )
    err_sent = err_sent.astype(jnp.bfloat16).reshape(dp_count, slot_cap, full_width)
    got_err = lax.all_to_all(err_sent, "dp", split_axis=0, concat_axis=0, tiled=True)
    errors = got_err.reshape(dp_count * slot_cap, full_width)
    recon = full.astype(jnp.bfloat16)
    grad_weights, grad_enc_bias = owner_grads(rows, errors, weights, pre, gate_lat, codes)
    grad_dec_bias = lax.psum(jnp.sum(err, axis=0), "dp")
    return (recon, grad_weights, grad_enc_bias, grad_dec_bias)


def solution(mesh):
    in_specs = (
        P("dp", "lat"),
        P("dp", None),
        P("dp", None),
        P(("dp", "lat"), None),
        P(("dp", "lat")),
        P("lat"),
    )
    out_specs = (P("dp", "lat"), P(("dp", "lat"), None), P(("dp", "lat")), P("lat"))
    return jax.shard_map(local, mesh=mesh, in_specs=in_specs, out_specs=out_specs, check_vma=False)
```

profile of v0, /device:TPU:0, one launch (start us, length us, event | category | flops | bytes accessed | tf_op | source)
XLA Modules:
  0.0 737.8 jit_solution(16515403187644802783)
XLA Ops:
  7.2 0.7 all-gather.3.cloned.1.call-update
  7.9 0.7 fusion.37
  8.6 0.7 add_select_fusion.2
  9.4 0.8 fusion.16
  10.2 0.7 fusion.12
  11.1 0.8 fusion.6
  12.7 8.3 %all-to-all-start.1 = ((bf16[16,32,2]{1,2,0:T(2,128)(2,1)}), bf16[16,32,2]{1,2,0:T(2,128)(2,1)S(1)}, u32[]{:S(2)}, u32[]{:S(2)}) async-start(bf16[16,32,2]{1,2,0:T(2,128)(2,1)} %convert_element_type.64), calls=%async_computation.1 | async-start | bytes 16384 | tf_op jit(solution)/shard_map/all_to_all | solution.py:85
  21.8 1.1 all-gather.3.cloned.1.call-done
  22.9 7.2 convolution_convert_fusion.2
  30.1 7.0 all-to-all-start
  37.3 158.9 %all-to-all-done = bf16[16,32,8192]{2,1,0:T(8,128)(2,1)} async-done(((bf16[16,32,8192]{2,1,0:T(8,128)(2,1)}), bf16[16,32,8192]{2,1,0:T(8,128)(2,1)}, u32[]{:S(2)}, u32[]{:S(2)}) %all-to-all-start) | async-done | bytes 8388640 | tf_op jit(solution)/shard_map/all_to_all | solution.py:84
  196.3 6.5 multiply_convert_fusion
  202.7 2.3 convolution_convert_fusion.1
  205.1 220.9 %all_to_all.20 = bf16[16,32,8192]{2,1,0:T(8,128)(2,1)S(1)} all-to-all(bf16[16,32,8192]{2,1,0:T(8,128)(2,1)S(1)} %bitcast.62), channel_id=1, replica_groups=mesh['dp'=16,'lat'=2] {'dp'}, dimensions={0} | all-to-all | bytes 16777216 | tf_op jit(solution)/shard_map/all_to_all | solution.py:92
  426.0 3.2 fusion.63
  429.5 10.7 %reduce-scatter.2.cloned.1.call-done = f32[128,4096]{1,0:T(8,128)} async-done(((f32[128,8192]{1,0:T(8,128)}), f32[128,4096]{1,0:T(8,128)}) %reduce-scatter.2.cloned.1.call-update) | async-done | bytes 2097168 | tf_op jit(solution)/shard_map/reduce_scatter | solution.py:98
  440.2 3.3 fusion.3
  443.5 12.0 %all-gather.5.cloned.1.call-done = bf16[128,8192]{1,0:T(8,128)(2,1)} async-done(((bf16[128,4096]{1,0:T(8,128)(2,1)}), bf16[128,8192]{1,0:T(8,128)(2,1)}) %all-gather.5.cloned.1.call-update) | async-done | bytes 2097168 | tf_op jit(solution)/shard_map/all_gather | solution.py:102
  455.5 7.3 convolution_convert_fusion
  462.8 6.8 all-to-all-start.3
  469.7 244.3 %psum.7 = f32[4096]{0:T(1024)} all-reduce(f32[4096]{0:T(1024)S(1)} %get-tuple-element.4), channel_id=1, replica_groups=mesh['dp'=16,'lat'=2] {'dp'}, use_global_device_ids=true, to_apply=%region_6.7 | all-reduce | flops 4096 | bytes 32768 | tf_op jit(solution)/shard_map/psum | solution.py:111
  713.9 4.8 fusion.65
  718.8 6.2 fusion.64
  725.0 6.3 fusion
  (29 shorter events, 2.5 us)
Async XLA Ops:
  7.2 189.1 %copy-start = (bf16[128,8192]{1,0:T(8,128)(2,1)S(1)}, bf16[128,8192]{1,0:T(8,128)(2,1)}, u32[]{:S(2)}) copy-start(bf16[128,8192]{1,0:T(8,128)(2,1)} %param.9) | copy-start | bytes 6291460
  7.2 15.7 %all-gather.3.cloned.1.call-start = ((), (), s32[]{:S(2)}) async-start(), calls=%async_computation.5 | async-start | bytes 3145728 | tf_op jit(solution)/shard_map/all_gather | solution.py:78
  12.7 17.4 %all-to-all-start.1 = ((bf16[16,32,2]{1,2,0:T(2,128)(2,1)}), bf16[16,32,2]{1,2,0:T(2,128)(2,1)S(1)}, u32[]{:S(2)}, u32[]{:S(2)}) async-start(bf16[16,32,2]{1,2,0:T(2,128)(2,1)} %convert_element_type.64), calls=%async_computation.1 | async-start | bytes 16384 | tf_op jit(solution)/shard_map/all_to_all | solution.py:85
  21.8 404.2 %copy-start.2 = (bf16[1,128,512]{2,0,1:T(2,128)(2,1)}, bf16[1,128,512]{2,0,1:T(2,128)(2,1)S(1)}, u32[]{:S(2)}) copy-start(bf16[1,128,512]{2,0,1:T(2,128)(2,1)S(1)} %fusion.45) | copy-start | bytes 393220
  30.1 166.2 %copy-start.4 = (f32[128]{0:T(128)S(1)}, f32[128]{0:T(128)}, u32[]{:S(2)}) copy-start(f32[128]{0:T(128)} %param.10) | copy-start | bytes 1540
  30.1 166.2 %all-to-all-start = ((bf16[16,32,8192]{2,1,0:T(8,128)(2,1)}), bf16[16,32,8192]{2,1,0:T(8,128)(2,1)}, u32[]{:S(2)}, u32[]{:S(2)}) async-start(bf16[16,32,8192]{2,1,0:T(8,128)(2,1)} %bitcast.59), calls=%async_computation | async-start | bytes 16777216 | tf_op jit(solution)/shard_map/all_to_all | solution.py:84
  37.0 403.1 %reduce-scatter.2.cloned.1.call-start = ((), (), s32[]{:S(2)}) async-start(), calls=%async_computation.6 | async-start | bytes 6291456 | tf_op jit(solution)/shard_map/reduce_scatter | solution.py:98
  429.2 10.9 %copy-start.1 = (bf16[128,4096]{1,0:T(8,128)(2,1)S(1)}, bf16[128,4096]{1,0:T(8,128)(2,1)}, u32[]{:S(2)}) copy-start(bf16[128,4096]{1,0:T(8,128)(2,1)} %param.6) | copy-start | bytes 3145732
  429.2 26.3 %all-gather.5.cloned.1.call-start = ((), (), s32[]{:S(2)}) async-start(), calls=%async_computation.7 | async-start | bytes 3145728 | tf_op jit(solution)/shard_map/all_gather | solution.py:102
  462.8 251.1 %all-to-all-start.3 = ((bf16[16,32,8192]{2,1,0:T(8,128)(2,1)}), bf16[16,32,8192]{2,1,0:T(8,128)(2,1)}, u32[]{:S(2)}, u32[]{:S(2)}) async-start(bf16[16,32,8192]{2,1,0:T(8,128)(2,1)} %bitcast.60), calls=%async_computation.4 | async-start | bytes 16777216 | tf_op jit(solution)/shard_map/all_to_all | solution.py:107
  713.9 4.8 copy-start.3
Sparse Core Ops, SparseCore 0:
  9.6 13.2 all-gather.2
  429.4 10.7 reduce-scatter.1
  443.6 11.8 all-gather.4
where the time goes:
time: 739 us; the launch traced here: 738 us
  blocking collectives  465 us (63%)
  waiting for transfers between devices  183 us (25%)
  matrix products  45.3 us (6%)
  starting transfers between devices  22.4 us (3%)
  between operations  13.9 us (2%)
    psum x1, blocking collectives, local(): grad_dec_bias = lax.psum(jnp.sum(err, axis=0), 'dp')  244 us
    all_to_all x1, blocking collectives, local(): lax.all_to_all(parts.reshape(dp_count, slot_cap, full_width), 'dp', split...  221 us
    all_to_all x1, waiting for transfers between devices, local(): lax.all_to_all(sent, 'dp', split_axis=0, concat_axis=0, tiled=True)  159 us
  transfers between devices with their start and end apart: 6, of which 4 were waited for; matrix products, arithmetic and copies ran while one was open for 2% of the time, Pallas kernels for 0%

commit v1 on v0

--- a/solution.py
+++ b/solution.py
@@ -108,7 +108,7 @@
     errors = got_err.reshape(dp_count * slot_cap, full_width)
     recon = full.astype(jnp.bfloat16)
     grad_weights, grad_enc_bias = owner_grads(rows, errors, weights, pre, gate_lat, codes)
-    grad_dec_bias = lax.psum(jnp.sum(err, axis=0), "dp")
+    grad_dec_bias = jnp.sum(lax.all_gather(jnp.sum(err, axis=0), "dp"), axis=0)
     return (recon, grad_weights, grad_enc_bias, grad_dec_bias)
 
 

time: 739 us -> 709 us (0.959); the launches traced: 738 us -> 697 us
  blocking collectives: 465 us -> 423 us
    psum x1 -> x0, blocking collectives: 244 us -> none  [local(): grad_dec_bias = lax.psum(jnp.sum(err, axis=0), 'dp')]
    all_gather x0 -> x1, blocking collectives: none -> 202 us  [local(): grad_dec_bias = jnp.sum(lax.all_gather(jnp.sum(err, axis=0), 'dp'), axis=0)]
where the time goes in v1:
time: 709 us; the launch traced here: 697 us
  blocking collectives  423 us (60%)
  waiting for transfers between devices  183 us (26%)
  matrix products  45.3 us (6%)
  starting transfers between devices  22.4 us (3%)
  between operations  13.9 us (2%)
  other arithmetic  7.82 us (1%)
    all_to_all x1, blocking collectives, local(): lax.all_to_all(parts.reshape(dp_count, slot_cap, full_width), 'dp', split...  221 us
    all_gather x1, blocking collectives, local(): grad_dec_bias = jnp.sum(lax.all_gather(jnp.sum(err, axis=0), 'dp'), axis=0)  202 us
    all_to_all x1, waiting for transfers between devices, local(): lax.all_to_all(sent, 'dp', split_axis=0, concat_axis=0, tiled=True)  159 us
  transfers between devices with their start and end apart: 6, of which 4 were waited for; matrix products, arithmetic and copies ran while one was open for 2% of the time, Pallas kernels for 0%

profile of v1, /device:TPU:0, one launch (start us, length us, event | category | flops | bytes accessed | tf_op | source)
XLA Modules:
  0.0 696.6 jit_solution(7459261461438892784)
XLA Ops:
  7.2 0.7 all-gather.4.cloned.1.call-update
  7.9 0.7 fusion.32
  8.6 0.7 add_select_fusion.2
  9.4 0.8 fusion.11
  10.2 0.7 fusion.7
  11.1 0.8 convolution_bitcast_fusion
  12.7 8.3 %all-to-all-start.1 = ((bf16[16,32,2]{1,2,0:T(2,128)(2,1)}), bf16[16,32,2]{1,2,0:T(2,128)(2,1)S(1)}, u32[]{:S(2)}, u32[]{:S(2)}) async-start(bf16[16,32,2]{1,2,0:T(2,128)(2,1)} %convert_element_type.64), calls=%async_computation.1 | async-start | bytes 16384 | tf_op jit(solution)/shard_map/all_to_all | solution.py:85
  21.8 1.1 all-gather.4.cloned.1.call-done
  22.9 7.2 %convolution_convert_fusion.2 = bf16[512,8192]{1,0:T(8,128)(2,1)} fusion(bf16[128,8192]{1,0:T(8,128)(2,1)} %all-gather.4.cloned.1.call-done, bf16[1,128,512]{2,0,1:T(2,128)(2,1)S(1)} %fusion.40), kind=kOutput, calls=%fused_computation.2 | convolution fusion | flops 1077936128 | bytes 10616832 | tf_op jit(solution)/shard_map/dot_general | solution.py:79
  30.1 7.0 %all-to-all-start = ((bf16[16,32,8192]{2,1,0:T(8,128)(2,1)}), bf16[16,32,8192]{2,1,0:T(8,128)(2,1)}, u32[]{:S(2)}, u32[]{:S(2)}) async-start(bf16[16,32,8192]{2,1,0:T(8,128)(2,1)} %bitcast.60), calls=%async_computation | async-start | bytes 16777216 | tf_op jit(solution)/shard_map/all_to_all | solution.py:84
  37.3 158.9 %all-to-all-done = bf16[16,32,8192]{2,1,0:T(8,128)(2,1)} async-done(((bf16[16,32,8192]{2,1,0:T(8,128)(2,1)}), bf16[16,32,8192]{2,1,0:T(8,128)(2,1)}, u32[]{:S(2)}, u32[]{:S(2)}) %all-to-all-start) | async-done | bytes 8388640 | tf_op jit(solution)/shard_map/all_to_all | solution.py:84
  196.3 6.5 multiply_convert_fusion
  202.7 2.3 convolution_convert_fusion.1
  205.1 220.9 %all_to_all.20 = bf16[16,32,8192]{2,1,0:T(8,128)(2,1)S(1)} all-to-all(bf16[16,32,8192]{2,1,0:T(8,128)(2,1)S(1)} %bitcast.63), channel_id=1, replica_groups=mesh['dp'=16,'lat'=2] {'dp'}, dimensions={0} | all-to-all | bytes 16777216 | tf_op jit(solution)/shard_map/all_to_all | solution.py:92
  426.0 3.2 fusion.58
  429.5 10.7 %reduce-scatter.2.cloned.1.call-done = f32[128,4096]{1,0:T(8,128)} async-done(((f32[128,8192]{1,0:T(8,128)}), f32[128,4096]{1,0:T(8,128)}) %reduce-scatter.2.cloned.1.call-update) | async-done | bytes 2097168 | tf_op jit(solution)/shard_map/reduce_scatter | solution.py:98
  440.2 3.3 fusion.1
  443.5 12.0 %all-gather.6.cloned.1.call-done = bf16[128,8192]{1,0:T(8,128)(2,1)} async-done(((bf16[128,4096]{1,0:T(8,128)(2,1)}), bf16[128,8192]{1,0:T(8,128)(2,1)}) %all-gather.6.cloned.1.call-update) | async-done | bytes 2097168 | tf_op jit(solution)/shard_map/all_gather | solution.py:102
  455.5 7.3 %convolution_convert_fusion = bf16[512,8192]{1,0:T(8,128)(2,1)} fusion(bf16[128,8192]{1,0:T(8,128)(2,1)} %all-gather.6.cloned.1.call-done, bf16[1,128,512]{2,0,1:T(2,128)(2,1)} %copy-done.2), kind=kOutput, calls=%fused_computation | convolution fusion | flops 1077936128 | bytes 10616832 | tf_op jit(solution)/shard_map/dot_general | solution.py:103
  462.8 6.8 all-to-all-start.3
  469.7 202.3 %all-gather = f32[65536]{0:T(1024)S(1)} all-gather(f32[4096]{0:T(1024)S(1)} %get-tuple-element.4), channel_id=2, replica_groups=mesh['dp'=16,'lat'=2] {'dp'}, dimensions={0}, use_global_device_ids=true | all-gather | bytes 278528 | tf_op jit(solution)/shard_map/all_gather | solution.py:111
  672.7 4.8 fusion.60
  677.5 6.2 fusion.59
  683.8 6.3 fusion
  (31 shorter events, 3.2 us)
Async XLA Ops:
  7.2 189.1 %copy-start = (bf16[128,8192]{1,0:T(8,128)(2,1)S(1)}, bf16[128,8192]{1,0:T(8,128)(2,1)}, u32[]{:S(2)}) copy-start(bf16[128,8192]{1,0:T(8,128)(2,1)} %param.9) | copy-start | bytes 6291460
  7.2 15.7 %all-gather.4.cloned.1.call-start = ((), (), s32[]{:S(2)}) async-start(), calls=%async_computation.5 | async-start | bytes 3145728 | tf_op jit(solution)/shard_map/all_gather | solution.py:78
  12.7 17.4 %all-to-all-start.1 = ((bf16[16,32,2]{1,2,0:T(2,128)(2,1)}), bf16[16,32,2]{1,2,0:T(2,128)(2,1)S(1)}, u32[]{:S(2)}, u32[]{:S(2)}) async-start(bf16[16,32,2]{1,2,0:T(2,128)(2,1)} %convert_element_type.64), calls=%async_computation.1 | async-start | bytes 16384 | tf_op jit(solution)/shard_map/all_to_all | solution.py:85
  21.8 404.2 %copy-start.2 = (bf16[1,128,512]{2,0,1:T(2,128)(2,1)}, bf16[1,128,512]{2,0,1:T(2,128)(2,1)S(1)}, u32[]{:S(2)}) copy-start(bf16[1,128,512]{2,0,1:T(2,128)(2,1)S(1)} %fusion.40) | copy-start | bytes 393220
  30.1 166.2 %copy-start.4 = (f32[128]{0:T(128)S(1)}, f32[128]{0:T(128)}, u32[]{:S(2)}) copy-start(f32[128]{0:T(128)} %param.10) | copy-start | bytes 1540
  30.1 166.2 %all-to-all-start = ((bf16[16,32,8192]{2,1,0:T(8,128)(2,1)}), bf16[16,32,8192]{2,1,0:T(8,128)(2,1)}, u32[]{:S(2)}, u32[]{:S(2)}) async-start(bf16[16,32,8192]{2,1,0:T(8,128)(2,1)} %bitcast.60), calls=%async_computation | async-start | bytes 16777216 | tf_op jit(solution)/shard_map/all_to_all | solution.py:84
  37.0 403.1 %reduce-scatter.2.cloned.1.call-start = ((), (), s32[]{:S(2)}) async-start(), calls=%async_computation.6 | async-start | bytes 6291456 | tf_op jit(solution)/shard_map/reduce_scatter | solution.py:98
  429.2 10.9 %copy-start.1 = (bf16[128,4096]{1,0:T(8,128)(2,1)S(1)}, bf16[128,4096]{1,0:T(8,128)(2,1)}, u32[]{:S(2)}) copy-start(bf16[128,4096]{1,0:T(8,128)(2,1)} %param.6) | copy-start | bytes 3145732
  429.2 26.3 %all-gather.6.cloned.1.call-start = ((), (), s32[]{:S(2)}) async-start(), calls=%async_computation.7 | async-start | bytes 3145728 | tf_op jit(solution)/shard_map/all_gather | solution.py:102
  462.8 209.9 %all-to-all-start.3 = ((bf16[16,32,8192]{2,1,0:T(8,128)(2,1)}), bf16[16,32,8192]{2,1,0:T(8,128)(2,1)}, u32[]{:S(2)}, u32[]{:S(2)}) async-start(bf16[16,32,8192]{2,1,0:T(8,128)(2,1)} %bitcast.61), calls=%async_computation.4 | async-start | bytes 16777216 | tf_op jit(solution)/shard_map/all_to_all | solution.py:107
  672.7 4.9 copy-start.3
Sparse Core Ops, SparseCore 0:
  9.6 13.2 all-gather.3
  429.4 10.7 reduce-scatter.1
  443.6 11.8 all-gather.5
